TPU v7x, 256 devices: a whole 4x4x8 slice. The times are simulated.
256 devices in a mesh: pipe: 2 (over core), seq: 4 (over x), tensor: 32 (over z, y).
Axes of the slice: x: 4, y: 4, z: 8, core: 2. Of those that a mesh axis runs over, the one named last changes fastest.
Arguments:
- token_ids: int32 [2, 768], P(None, 'seq'), may hold values from 0 to 511
- embed_table: bfloat16 [512, 8192], P(None, 'tensor'), may hold values from -24 to 24
- in_proj: bfloat16 [2, 8192, 3, 4096], P('pipe', None, None, 'tensor'), may hold values from -0.0625 to 0.0625
- feat_taps: float32 [2, 3, 3, 4096], P('pipe', None, None, 'tensor'), may hold values from -3 to 3
- se_taps: float32 [7, 4096], P(None, 'tensor'), may hold values from -2 to 2
- mr_taps: float32 [128, 4096], P(None, 'tensor'), may hold values from -0.6 to 0.6
- out_proj: bfloat16 [2, 4096, 8192], P('pipe', 'tensor'), may hold values from -0.1875 to 0.1875
- norm_gain: bfloat16 [2, 8192], P('pipe', 'tensor'), may hold values from 0.25 to 1.75
Outputs:
- segment_out: bfloat16 [2, 2, 768, 8192], P('pipe', None, 'seq', 'tensor')
All inputs are finite; a program needn't handle non-finite values.
Results may differ from a plain program's by a relative error of at most 0.023.
Values may be sent and summed in bfloat16 or wider, within the bound.
No kernel may reach another device: no remote copies, remote signals or barrier semaphores. Data moves between devices by JAX's collectives and lax.ppermute only.
A program may use at most 64 MiB of HBM per device.

v0:
```python
import jax
import jax.numpy as jnp
from jax import lax
from jax.sharding import PartitionSpec as P

VOCAB = 512
KL = 128
KS = 7
KF = 3
SEGMENTS = 2
HALO = 129
epsilon = 1e-06


def from_behind(value, axis, steps):
    count = lax.axis_size(axis)
    pairs = [(source, (source + steps) % count) for source in range(count)]
    return lax.ppermute(value, axis, pairs)


def passed_along(value, axis, steps):
    count = lax.axis_size(axis)
    first, last = (max(0, -steps), min(count, count - steps))
    return lax.ppermute(value, axis, [(source, source + steps) for source in range(first, last)])


def project(stream, w_flat, gain_cols):
    gathered, gain_all = (
        lax.all_gather(stream, "tensor", axis=2, tiled=True),
        lax.all_gather(gain_cols, "tensor", axis=1, tiled=True),
    )
    values = gathered.astype(jnp.float32)
    inv_rms = lax.rsqrt(jnp.mean(values * values, axis=2, keepdims=True) + epsilon)
    normed = (values * inv_rms * gain_all[0].astype(jnp.float32)).astype(jnp.bfloat16)
    projected = jnp.einsum("snd,dk->snk", normed, w_flat, preferred_element_type=jnp.float32)
    return projected.astype(jnp.bfloat16)


def send_tails(projected):
    row_count = projected.shape[1]
    chan_local = projected.shape[2] // 3
    kv_tail = projected[:, row_count - HALO :, chan_local:]
    q_tail = projected[:, row_count - (KF - 1) :, :chan_local]
    return from_behind((kv_tail, q_tail), "seq", 1)


def hand_over(result):
    return passed_along(result, "pipe", 1)


def mixing(stream, projected, kv_prev, q_prev, feat_local, long_taps, w_down):
    row_count = projected.shape[1]
    chan_local = projected.shape[2] // 3
    q_all = jnp.concatenate([q_prev, projected[:, :, :chan_local]], axis=1).astype(jnp.float32)
    kv_all = jnp.concatenate([kv_prev, projected[:, :, chan_local:]], axis=1).astype(jnp.float32)
    q_taps = feat_local[0, :, 0, :]
    kv_taps = feat_local[0, :, 1:, :].reshape(KF, 2 * chan_local)
    kv_span = KL - 1 + row_count
    q_feat = jnp.zeros((projected.shape[0], row_count, chan_local), jnp.float32)
    kv_feat = jnp.zeros((projected.shape[0], kv_span, 2 * chan_local), jnp.float32)
    for tap_index in range(KF):
        offset = KF - 1 - tap_index
        q_feat = q_feat + q_taps[tap_index] * q_all[:, offset : offset + row_count]
        kv_feat = kv_feat + kv_taps[tap_index] * kv_all[:, offset : offset + kv_span]
    gated_kv = kv_feat[:, :, :chan_local] * kv_feat[:, :, chan_local:]

    def add_tap(tap_index, running):
        shifted = lax.dynamic_slice_in_dim(gated_kv, KL - 1 - tap_index, row_count, 1)
        return running + long_taps[tap_index] * shifted

    filtered = lax.fori_loop(0, KL, add_tap, jnp.zeros_like(q_feat))
    y_out = (q_feat * filtered).astype(jnp.bfloat16)
    partial_terms = jnp.einsum("snc,cd->snd", y_out, w_down[0], preferred_element_type=jnp.float32)
    mixed = lax.psum_scatter(
        partial_terms.astype(jnp.bfloat16), "tensor", scatter_dimension=2, tiled=True
    ).astype(jnp.float32)
    return (stream.astype(jnp.float32) + mixed).astype(jnp.bfloat16)


def local(token_ids, embed_table, in_proj, feat_taps, se_taps, mr_taps, out_proj, norm_gain):
    section = lax.axis_index("pipe")
    shard_pos = lax.axis_index("seq")
    lead_segment = section == 0
    padded_se = jnp.concatenate(
        [se_taps, jnp.zeros((KL - KS, se_taps.shape[1]), jnp.float32)], axis=0
    )
    long_taps = jnp.where(lead_segment, padded_se, mr_taps)
    w_flat = in_proj[0].reshape(in_proj.shape[1], -1)
    vocab_ids = jnp.arange(VOCAB, dtype=jnp.int32)
    one_hot = (token_ids[:, :, None] == vocab_ids[None, None, :]).astype(jnp.bfloat16)
    embedded = jnp.einsum(
        "snv,vd->snd", one_hot, embed_table, preferred_element_type=jnp.float32
    ).astype(jnp.bfloat16)
    current = jnp.where(lead_segment, embedded, jnp.zeros_like(embedded))
    outputs = []
    for step_index in range(SEGMENTS):
        projected = project(current, w_flat, norm_gain)
        kv_recv, q_recv = send_tails(projected)
        kv_earlier = jnp.concatenate([jnp.zeros_like(kv_recv[:1]), kv_recv[:-1]], axis=0)
        q_earlier = jnp.concatenate([jnp.zeros_like(q_recv[:1]), q_recv[:-1]], axis=0)
        kv_prev = jnp.where(shard_pos == 0, kv_earlier, kv_recv)
        q_prev = jnp.where(shard_pos == 0, q_earlier, q_recv)
        result = mixing(current, projected, kv_prev, q_prev, feat_taps, long_taps, out_proj)
        outputs.append(result)
        if step_index + 1 < SEGMENTS:
            current = hand_over(result)
    final_out = lax.dynamic_index_in_dim(jnp.stack(outputs, axis=0), section, 0, keepdims=True)
    return final_out


def solution(mesh):
    return jax.shard_map(
        local,
        mesh=mesh,
        in_specs=(
            P(None, "seq"),
            P(None, "tensor"),
            P("pipe", None, None, "tensor"),
            P("pipe", None, None, "tensor"),
            P(None, "tensor"),
            P(None, "tensor"),
            P("pipe", "tensor", None),
            P("pipe", "tensor"),
        ),
        out_specs=P("pipe", None, "seq", "tensor"),
        check_vma=False,
    )
```

profile of v0, /device:TPU:4, one launch (start us, length us, event | category | flops | bytes accessed | tf_op | source)
XLA Modules:
  0.0 731.5 jit_solution(4473578818724126440)
XLA Ops:
  6.5 2.1 fusion.22
  8.8 8.7 %copy.9 = bf16[1,8192,3,128]{1,3,2,0:T(8,128)(2,1)} copy(bf16[1,8192,3,128]{3,1,2,0:T(8,128)(2,1)} %param.14) | data formatting | bytes 12582912 | tf_op args[2]
  17.5 46.2 %all_gather.11 = bf16[1,8192]{1,0:T(2,128)(2,1)S(1)} all-gather(bf16[1,256]{1,0:T(2,128)(2,1)S(1)} %copy-done.9), channel_id=1, replica_groups=mesh['pipe'=2,'seq'=4,'tensor'=32] {'tensor'}, dimensions={1}, use_global_device_ids=true | all-gather | bytes 16896 | tf_op jit(solution)/shard_map/all_gather | solution.py:30
  63.8 41.7 %all-gather.3.cloned.1.call-done = bf16[2,192,8192]{2,1,0:T(8,128)(2,1)} async-done(((bf16[2,192,256]{2,1,0:T(8,128)(2,1)}), bf16[2,192,8192]{2,1,0:T(8,128)(2,1)}) %all-gather.3.cloned.1.call-update) | async-done | bytes 6291472 | tf_op jit(solution)/shard_map/all_gather | solution.py:29
  105.5 4.3 fusion
  110.1 5.8 fusion.16
  115.9 1.2 collective-permute-start
  117.9 1.7 collective-permute-done
  119.6 2.8 collective-permute-done.1
  122.7 16.4 %while.32 = (s32[]{:T(128)}, f32[2,192,128]{2,1,0:T(8,128)S(1)}, f32[128,128]{1,0:T(8,128)S(1)}, f32[2,319,128]{2,1,0:T(8,128)S(1)}, s32[]{:T(128)}, /*index=5*/s32[]{:T(128)}, s32[]{:T(128)}, s32[]{:T(128)}) while((s32[]{:T(128)}, f32[2,192,128]{2,1,0:T(8,128)S(1)}, f32[128,128]{1,0:T(8,128)S(1)}, f32[2,319,128]{2,1,0:T(8,128)S(1)}, ...), condition=%wide.region_2.3_spmd.clone, body=%wide.region_1.2_spmd.clone.sunk | while | flops 147463 | bytes 591509 | solution.py:71
  139.2 4.4 convolution_convert_fusion.1
  143.7 223.0 %reduce-scatter.3.cloned.1.call-done = bf16[2,192,256]{2,1,0:T(8,128)(2,1)} async-done(((bf16[2,192,8192]{2,1,0:T(8,128)(2,1)}), bf16[2,192,256]{2,1,0:T(8,128)(2,1)}) %reduce-scatter.3.cloned.1.call-update) | async-done | bytes 196624 | tf_op jit(solution)/shard_map/reduce_scatter | solution.py:74
  366.7 1.0 add_convert_fusion.1
  367.7 1.3 collective-permute-start.2
  369.0 1.0 collective-permute-done.2
  370.9 90.8 %all-gather.5.cloned.1.call-done = bf16[2,192,8192]{2,1,0:T(8,128)(2,1)} async-done(((bf16[2,192,256]{2,1,0:T(8,128)(2,1)}), bf16[2,192,8192]{2,1,0:T(8,128)(2,1)}) %all-gather.5.cloned.1.call-update) | async-done | bytes 6291472 | tf_op jit(solution)/shard_map/all_gather | solution.py:29
  461.8 4.3 fusion.3
  466.4 6.2 fusion.19
  472.6 1.3 collective-permute-start.3
  474.6 1.7 collective-permute-done.3
  476.3 2.8 collective-permute-done.4
  479.5 16.4 %while.33 = (s32[]{:T(128)}, f32[2,192,128]{2,1,0:T(8,128)S(1)}, f32[128,128]{1,0:T(8,128)S(1)}, f32[2,319,128]{2,1,0:T(8,128)S(1)}, s32[]{:T(128)}, /*index=5*/s32[]{:T(128)}, s32[]{:T(128)}, s32[]{:T(128)}) while((s32[]{:T(128)}, f32[2,192,128]{2,1,0:T(8,128)S(1)}, f32[128,128]{1,0:T(8,128)S(1)}, f32[2,319,128]{2,1,0:T(8,128)S(1)}, ...), condition=%wide.region_6.7_spmd.clone, body=%wide.region_5.6_spmd.clone.sunk | while | flops 147463 | bytes 591509 | solution.py:71
  495.9 4.5 convolution_convert_fusion
  500.4 222.8 %reduce-scatter.5.cloned.1.call-done = bf16[2,192,256]{2,1,0:T(8,128)(2,1)} async-done(((bf16[2,192,8192]{2,1,0:T(8,128)(2,1)}), bf16[2,192,256]{2,1,0:T(8,128)(2,1)}) %reduce-scatter.5.cloned.1.call-update) | async-done | bytes 196624 | tf_op jit(solution)/shard_map/reduce_scatter | solution.py:74
  (576 shorter events, 29.0 us)
Async XLA Ops:
  6.5 132.6 %copy-start = (bf16[1,128,8192]{2,1,0:T(8,128)(2,1)S(1)}, bf16[1,128,8192]{2,1,0:T(8,128)(2,1)}, u32[]{:S(2)}) copy-start(bf16[1,128,8192]{2,1,0:T(8,128)(2,1)} %param.18) | copy-start | bytes 6291460
  6.5 99.0 %all-gather.3.cloned.1.call-start = ((), (), s32[]{:S(2)}) async-start(), calls=%async_computation.2 | async-start | bytes 6488064 | tf_op jit(solution)/shard_map/all_gather | solution.py:29
  8.7 8.8 %copy-start.9 = (bf16[1,256]{1,0:T(2,128)(2,1)S(1)}, bf16[1,256]{1,0:T(2,128)(2,1)}, u32[]{:S(2)}) copy-start(bf16[1,256]{1,0:T(2,128)(2,1)} %param.19) | copy-start | bytes 1540
  8.7 55.1 %copy-start.7 = (f32[1,3,3,128]{3,0,2,1:T(1,128)S(1)}, f32[1,3,3,128]{3,0,2,1:T(1,128)}, u32[]{:S(2)}) copy-start(f32[1,3,3,128]{3,0,2,1:T(1,128)} %param.15) | copy-start | bytes 13828
  8.7 55.1 %copy-start.6 = (f32[128,128]{1,0:T(8,128)S(1)}, f32[128,128]{1,0:T(8,128)}, u32[]{:S(2)}) copy-start(f32[128,128]{1,0:T(8,128)} %param.17) | copy-start | bytes 196612
  8.7 55.1 %copy-start.8 = (f32[7,128]{1,0:T(8,128)S(1)}, f32[7,128]{1,0:T(8,128)}, u32[]{:S(2)}) copy-start(f32[7,128]{1,0:T(8,128)} %param.16) | copy-start | bytes 10756
  8.7 358.0 %reduce-scatter.3.cloned.1.call-start = ((), (), s32[]{:S(2)}) async-start(), calls=%async_computation.3 | async-start | bytes 6488064 | tf_op jit(solution)/shard_map/reduce_scatter | solution.py:74
  105.5 4.6 copy-start.1
  115.9 3.6 collective-permute-start
  117.3 5.1 collective-permute-start.1
  139.2 227.5 %copy-start.3 = (bf16[2,192,256]{2,1,0:T(8,128)(2,1)S(1)}, bf16[2,192,256]{2,1,0:T(8,128)(2,1)}, u32[]{:S(2)}) copy-start(bf16[2,192,256]{2,1,0:T(8,128)(2,1)} %fusion.22) | copy-start | bytes 589828
  143.6 318.2 %all-gather.5.cloned.1.call-start = ((), (), s32[]{:S(2)}) async-start(), calls=%async_computation.4 | async-start | bytes 6488064 | tf_op jit(solution)/shard_map/all_gather | solution.py:29
  367.7 2.4 collective-permute-start.2
  370.0 0.7 copy-start.4
  370.7 352.5 %reduce-scatter.5.cloned.1.call-start = ((), (), s32[]{:S(2)}) async-start(), calls=%async_computation.5 | async-start | bytes 6488064 | tf_op jit(solution)/shard_map/reduce_scatter | solution.py:74
  461.8 4.6 copy-start.2
  472.6 3.6 collective-permute-start.3
  474.0 5.1 collective-permute-start.4
  495.9 227.3 %copy-start.5 = (bf16[2,192,256]{2,1,0:T(8,128)(2,1)S(1)}, bf16[2,192,256]{2,1,0:T(8,128)(2,1)}, u32[]{:S(2)}) copy-start(bf16[2,192,256]{2,1,0:T(8,128)(2,1)} %copy-done.4) | copy-start | bytes 589828
Sparse Core Ops, SparseCore 0:
  9.8 95.6 all-gather.2
  143.7 222.8 reduce-scatter.2
  370.8 90.9 all-gather.4
  500.5 222.6 reduce-scatter.4
where the time goes:
time: 732 us; the launch traced here: 731 us
  waiting for transfers between devices  588 us (80%)
  blocking collectives  46.2 us (6%)
  other arithmetic  32.8 us (4%)
  matrix products  23.1 us (3%)
  between operations  13.4 us (2%)
  local copies, waits for them, and re-layouts  12.7 us (2%)
  loops' own time  9.56 us (1%)
    reduce_scatter x2, waiting for transfers between devices, mixing(): lax.psum_scatter(partial_terms.astype(jnp.bfloat16), 'tensor', scatter_di...  446 us
    all_gather x2, waiting for transfers between devices, project(): lax.all_gather(stream, 'tensor', axis=2, tiled=True)  132 us
    all_gather x1, blocking collectives, project(): lax.all_gather(gain_cols, 'tensor', axis=1, tiled=True)  46.2 us
    add x256, other arithmetic, add_tap(): return running + long_taps[tap_index] * shifted  20.9 us
  transfers between devices with their start and end apart: 9, of which 9 were waited for; matrix products, arithmetic and copies ran while one was open for 1% of the time, Pallas kernels for 0%

commit v1 on v0

--- a/solution.py
+++ b/solution.py
@@ -26,7 +26,9 @@
 
 def project(stream, w_flat, gain_cols):
     gathered, gain_all = (
-        lax.all_gather(stream, "tensor", axis=2, tiled=True),
+        jnp.concatenate(
+            lax.all_to_all(jnp.stack([stream] * lax.axis_size("tensor")), "tensor", 0, 0), axis=2
+        ),
         lax.all_gather(gain_cols, "tensor", axis=1, tiled=True),
     )
     values = gathered.astype(jnp.float32)

time: 732 us -> 896 us (1.22)
  blocking collectives: 46.2 us -> 325 us
  waiting for transfers between devices: 588 us -> 452 us
  starting transfers between devices: 5.37 us -> 16.9 us
    all_to_all x0 -> x1, blocking collectives: none -> 147 us  [project(): lax.all_to_all(jnp.stack([stream] * lax.axis_size('tensor')), 'tensor', 0...]
    all_gather x2 -> x0, waiting for transfers between devices: 132 us -> none  [project(): lax.all_gather(stream, 'tensor', axis=2, tiled=True)]
    all_gather x1, blocking collectives: 46.2 us -> 178 us  [project(): lax.all_gather(gain_cols, 'tensor', axis=1, tiled=True)]
    all_to_all x0 -> x1, starting transfers between devices: none -> 11.7 us  [project(): lax.all_to_all(jnp.stack([stream] * lax.axis_size('tensor')), 'tensor', 0...]
  transfers between devices with their start and end apart: 9 -> 8, of which waited for: 9 -> 7; matrix products, arithmetic and copies ran while one was open for 1% -> 1% of each run, Pallas kernels for 0% -> 0%
where the time goes in v1:
time: 896 us
  waiting for transfers between devices  452 us (50%)
  blocking collectives  325 us (36%)
  other arithmetic  37.2 us (4%)
  matrix products  21.5 us (2%)
  local copies, waits for them, and re-layouts  19.8 us (2%)
  starting transfers between devices  16.9 us (2%)
  between operations  13.7 us (2%)
  loops' own time  9.56 us (1%)
    reduce_scatter x2, waiting for transfers between devices, mixing(): lax.psum_scatter(partial_terms.astype(jnp.bfloat16), 'tensor', scatter_di...  442 us
    all_gather x1, blocking collectives, project(): lax.all_gather(gain_cols, 'tensor', axis=1, tiled=True)  178 us
    all_to_all x1, blocking collectives, project(): lax.all_to_all(jnp.stack([stream] * lax.axis_size('tensor')), 'tensor', 0...  147 us
    add x256, other arithmetic, add_tap(): return running + long_taps[tap_index] * shifted  20.9 us
  transfers between devices with their start and end apart: 8, of which 7 were waited for; matrix products, arithmetic and copies ran while one was open for 1% of the time, Pallas kernels for 0%

profile of v1, /device:TPU:4, one launch (start us, length us, event | category | flops | bytes accessed | tf_op | source)
XLA Modules:
  0.0 895.8 jit_solution(12490926454951824374)
XLA Ops:
  6.5 1.4 fusion.10
  8.0 3.4 stack.10
  11.3 11.7 %all-to-all-start = ((bf16[32,2,192,256]{3,2,1,0:T(8,128)(2,1)}), bf16[32,2,192,256]{3,2,1,0:T(8,128)(2,1)}, u32[]{:S(2)}, u32[]{:S(2)}) async-start(bf16[32,2,192,256]{3,2,1,0:T(8,128)(2,1)} %stack.10), calls=%async_computation | async-start | bytes 12582912 | tf_op jit(solution)/shard_map/all_to_all | solution.py:30
  23.1 177.7 %all_gather.4 = bf16[1,8192]{1,0:T(2,128)(2,1)S(1)} all-gather(bf16[1,256]{1,0:T(2,128)(2,1)S(1)} %copy-done.4), channel_id=1, replica_groups=mesh['pipe'=2,'seq'=4,'tensor'=32] {'tensor'}, dimensions={1}, use_global_device_ids=true | all-gather | bytes 16896 | tf_op jit(solution)/shard_map/all_gather | solution.py:32
  201.0 8.8 copy.16
  209.8 4.3 fusion
  214.1 4.9 fusion.7
  219.1 3.5 copy.24
  222.5 5.6 convolution_convert_fusion.3
  230.1 1.7 collective-permute-done
  231.8 2.8 collective-permute-done.1
  234.9 16.4 %while.32 = (s32[]{:T(128)}, f32[2,192,128]{2,1,0:T(8,128)S(1)}, f32[128,128]{1,0:T(8,128)S(1)}, f32[2,319,128]{2,1,0:T(8,128)S(1)}, s32[]{:T(128)}, /*index=5*/s32[]{:T(128)}, s32[]{:T(128)}, s32[]{:T(128)}) while((s32[]{:T(128)}, f32[2,192,128]{2,1,0:T(8,128)S(1)}, f32[128,128]{1,0:T(8,128)S(1)}, f32[2,319,128]{2,1,0:T(8,128)S(1)}, ...), condition=%wide.region_2.3_spmd.clone, body=%wide.region_1.2_spmd.clone.sunk | while | flops 147463 | bytes 591509 | solution.py:73
  251.4 4.5 convolution_convert_fusion.1
  255.9 221.1 %reduce-scatter.3.cloned.1.call-done = bf16[2,192,256]{2,1,0:T(8,128)(2,1)} async-done(((bf16[2,192,8192]{2,1,0:T(8,128)(2,1)}), bf16[2,192,256]{2,1,0:T(8,128)(2,1)}) %reduce-scatter.3.cloned.1.call-update) | async-done | bytes 196624 | tf_op jit(solution)/shard_map/reduce_scatter | solution.py:76
  478.0 1.3 collective-permute-start.2
  481.1 147.5 %all_to_all.10 = bf16[32,2,192,256]{3,2,1,0:T(8,128)(2,1)S(1)} all-to-all(bf16[32,2,192,256]{3,2,1,0:T(8,128)(2,1)S(1)} %stack.12), channel_id=1, replica_groups=mesh['pipe'=2,'seq'=4,'tensor'=32] {'tensor'}, dimensions={0} | all-to-all | bytes 12582912 | tf_op jit(solution)/shard_map/all_to_all | solution.py:30
  628.6 1.3 fusion.3
  629.9 2.3 fusion.6
  633.1 5.6 convolution_convert_fusion.2
  640.6 1.7 collective-permute-done.3
  642.4 2.8 collective-permute-done.4
  645.5 16.4 %while.33 = (s32[]{:T(128)}, f32[2,192,128]{2,1,0:T(8,128)S(1)}, f32[128,128]{1,0:T(8,128)S(1)}, f32[2,319,128]{2,1,0:T(8,128)S(1)}, s32[]{:T(128)}, /*index=5*/s32[]{:T(128)}, s32[]{:T(128)}, s32[]{:T(128)}) while((s32[]{:T(128)}, f32[2,192,128]{2,1,0:T(8,128)S(1)}, f32[128,128]{1,0:T(8,128)S(1)}, f32[2,319,128]{2,1,0:T(8,128)S(1)}, ...), condition=%wide.region_6.7_spmd.clone, body=%wide.region_5.6_spmd.clone.sunk | while | flops 147463 | bytes 591509 | solution.py:73
  661.9 4.5 convolution_convert_fusion
  666.4 220.8 %reduce-scatter.5.cloned.1.call-done = bf16[2,192,256]{2,1,0:T(8,128)(2,1)} async-done(((bf16[2,192,8192]{2,1,0:T(8,128)(2,1)}), bf16[2,192,256]{2,1,0:T(8,128)(2,1)}) %reduce-scatter.5.cloned.1.call-update) | async-done | bytes 196624 | tf_op jit(solution)/shard_map/reduce_scatter | solution.py:76
  (575 shorter events, 33.5 us)
Async XLA Ops:
  6.5 244.9 %copy-start = (bf16[1,128,8192]{2,1,0:T(8,128)(2,1)S(1)}, bf16[1,128,8192]{2,1,0:T(8,128)(2,1)}, u32[]{:S(2)}) copy-start(bf16[1,128,8192]{2,1,0:T(8,128)(2,1)} %param.18) | copy-start | bytes 6291460
  11.3 11.8 %copy-start.4 = (bf16[1,256]{1,0:T(2,128)(2,1)S(1)}, bf16[1,256]{1,0:T(2,128)(2,1)}, u32[]{:S(2)}) copy-start(bf16[1,256]{1,0:T(2,128)(2,1)} %param.19) | copy-start | bytes 1540
  11.3 198.5 %all-to-all-start = ((bf16[32,2,192,256]{3,2,1,0:T(8,128)(2,1)}), bf16[32,2,192,256]{3,2,1,0:T(8,128)(2,1)}, u32[]{:S(2)}, u32[]{:S(2)}) async-start(bf16[32,2,192,256]{3,2,1,0:T(8,128)(2,1)} %stack.10), calls=%async_computation | async-start | bytes 12582912 | tf_op jit(solution)/shard_map/all_to_all | solution.py:30
  23.1 454.0 %reduce-scatter.3.cloned.1.call-start = ((), (), s32[]{:S(2)}) async-start(), calls=%async_computation.4 | async-start | bytes 6488064 | tf_op jit(solution)/shard_map/reduce_scatter | solution.py:76
  201.0 8.8 copy-start.2
  201.0 8.8 copy-start.1
  201.0 8.8 copy-start.3
  209.8 12.7 %slice-start = ((s8[6291456]{0:T(1024)(128)(4,1)}), s8[4194304]{0:T(1024)(128)(4,1)S(1)}, s32[]{:S(2)}) async-start(s8[6291456]{0:T(1024)(128)(4,1)} %bitcast.46), calls=%async_computation.6 | async-start | bytes 8388608
  214.1 8.4 slice-start.1
  228.1 3.6 collective-permute-start
  229.5 5.1 collective-permute-start.1
  255.9 631.3 %reduce-scatter.5.cloned.1.call-start = ((), (), s32[]{:S(2)}) async-start(), calls=%async_computation.5 | async-start | bytes 6488064 | tf_op jit(solution)/shard_map/reduce_scatter | solution.py:76
  478.0 2.4 collective-permute-start.2
  638.6 3.7 collective-permute-start.3
  640.0 5.1 collective-permute-start.4
Sparse Core Ops, SparseCore 0:
  256.0 220.9 reduce-scatter.2
  666.5 220.6 reduce-scatter.4
